TPU v7x, 512 devices: a whole 4x4x16 slice. The times are simulated.
512 devices in a mesh: dp: 4 (over x), seq: 8 (over z_lo), tensor: 16 (over z_hi, y, core).
Axes of the slice: x: 4, y: 4, z: 16 (z_hi: 2, z_lo: 8; z = z_hi * 8 + z_lo), core: 2. Of those that a mesh axis runs over, the one named last changes fastest.
Arguments:
- features: bfloat16 [4096, 4096], P(('dp', 'seq'), 'tensor'), parts along dimension 0, may hold values from -6 to 6
- in_weight: bfloat16 [4096, 3, 4096], P('seq', None, 'tensor'), may hold values from -0.09375 to 0.09375
- short_taps: float32 [3, 7, 4096], P(None, None, 'tensor'), may hold values from -2.5 to 2.5
- decay_rates: float32 [16, 4096], P(None, 'tensor'), may hold values from 0.00048828125 to 0.1
- residues: float32 [16, 4096], P(None, 'tensor'), may hold values from -1.5 to 1.5
- skip_gain: float32 [4096], P('tensor'), may hold values from 0.5 to 1.5
- out_weight: bfloat16 [4096, 4096], P(None, 'tensor'), may hold values from -0.09375 to 0.09375
Outputs:
- mixed: bfloat16 [4096, 4096], P(('dp', 'seq'), 'tensor'), parts along dimension 0
There are 4 independent parts, one for each index of `dp`. A program takes and returns all parts, laid end to end along the dimension named above; an argument that names none is the same for every part. Nothing has to cross between parts.
All inputs are finite; a program needn't handle non-finite values.
Results may differ from a plain program's by a relative error of at most 0.007.
Values may be sent and summed in bfloat16 or wider, within the bound.
No kernel may reach another device: no remote copies, remote signals or barrier semaphores. Data moves between devices by JAX's collectives and lax.ppermute only.
A program may use at most 64 MiB of HBM per device.

v0:
```python
import jax
import jax.numpy as jnp
from jax import lax
from jax.sharding import PartitionSpec as P

precise = lax.Precision.HIGHEST
block_len = 64


def passed_along(value, axis, steps):
    count = lax.axis_size(axis)
    leading, last = (max(0, -steps), min(count, count - steps))
    return lax.ppermute(value, axis, [(source, source + steps) for source in range(leading, last)])


def body(features, in_weight, short_taps, decay_rates, residues, skip_gain, out_weight):
    tok_rows = features.shape[0]
    channels = in_weight.shape[2]
    taps_count = short_taps.shape[1]
    whole_feats = lax.all_gather(features, "tensor", axis=1, tiled=True)
    piece = lax.all_gather(in_weight, "seq", axis=0, tiled=True)
    count = piece.shape[0]
    projected = jnp.dot(
        whole_feats, piece.reshape(count, 3 * channels), preferred_element_type=jnp.float32
    )
    projected = projected.astype(jnp.bfloat16).reshape(tok_rows, 3, channels)
    rim_rows = taps_count - 1
    earlier = passed_along(projected[tok_rows - rim_rows :], "seq", 1)
    extended = jnp.concatenate([earlier, projected], axis=0).astype(jnp.float32)
    short = jnp.zeros((tok_rows, 3, channels), jnp.float32)
    for offset_lag in range(taps_count):
        short = (
            short
            + short_taps[:, offset_lag, :][None]
            * extended[rim_rows - offset_lag : rim_rows - offset_lag + tok_rows]
        )
    product = short[:, 1, :] * short[:, 2, :]
    blocks = tok_rows // block_len
    pieces = product.reshape(blocks, block_len, channels)
    amplitude = residues * jnp.sqrt(2.0 * decay_rates)
    offsets = jnp.arange(block_len).astype(jnp.float32)
    falloff = jnp.exp(-decay_rates[:, None, :] * offsets[None, :, None])
    kernel = jnp.einsum("mc,mtc->tc", amplitude, falloff, precision=precise)
    lag_grid = jnp.arange(block_len)[:, None] - jnp.arange(block_len)[None, :]
    select = (lag_grid[:, :, None] == jnp.arange(block_len)[None, None, :]).astype(jnp.float32)
    toeplitz = jnp.einsum("tsk,kc->tsc", select, kernel, precision=precise)
    inner = jnp.einsum("tsc,bsc->btc", toeplitz, pieces, precision=precise)
    toward_end = jnp.exp(-decay_rates[:, None, :] * (block_len - offsets)[None, :, None])
    block_sums = jnp.einsum("msc,bsc->bmc", toward_end, pieces, precision=precise)
    block_index = jnp.arange(blocks).astype(jnp.float32)
    carry_over = jnp.exp(
        -decay_rates[None] * (block_len * (blocks - 1 - block_index))[:, None, None]
    )
    device_sum = jnp.sum(carry_over * block_sums, axis=0)
    place = lax.axis_index("seq")
    gathered_sums = lax.all_gather(device_sum, "seq")
    earlier_count = jnp.arange(gathered_sums.shape[0])
    distance = (place - 1 - earlier_count).astype(jnp.float32)
    weight = jnp.where(
        (earlier_count < place)[:, None, None],
        jnp.exp(-decay_rates[None] * (float(tok_rows) * jnp.maximum(distance, 0.0))[:, None, None]),
        0.0,
    )
    entering = jnp.sum(weight * gathered_sums, axis=0)
    step_decay = jnp.exp(-decay_rates * float(block_len))

    def advance(state, block_sum):
        return (step_decay * state + block_sum, state)

    final_state, starts = lax.scan(advance, entering, block_sums)
    outer = jnp.einsum("mic,bmc->bic", amplitude[:, None, :] * falloff, starts, precision=precise)
    conv = (inner + outer).reshape(tok_rows, channels)
    gated = (short[:, 0, :] * (conv + skip_gain[None, :] * product)).astype(jnp.bfloat16)
    mixed = jnp.dot(
        lax.all_gather(gated, "tensor", axis=1, tiled=True),
        out_weight,
        preferred_element_type=jnp.float32,
    )
    return mixed.astype(jnp.bfloat16)


def solution(mesh):
    in_specs = (
        P(("dp", "seq"), "tensor"),
        P("seq", None, "tensor"),
        P(None, None, "tensor"),
        P(None, "tensor"),
        P(None, "tensor"),
        P("tensor"),
        P(None, "tensor"),
    )
    out_specs = P(("dp", "seq"), "tensor")
    return jax.shard_map(body, mesh=mesh, in_specs=in_specs, out_specs=out_specs, check_vma=False)
```

profile of v0, /device:TPU:1, one launch (start us, length us, event | category | flops | bytes accessed | tf_op | source)
XLA Modules:
  0.0 405.0 jit_solution(2613455563154956939)
XLA Ops:
  6.6 0.7 all-gather.5.cloned.1.call-update
  7.3 2.3 copy.59
  10.0 1.6 multiply_reduce_fusion
  11.7 3.8 fusion.5
  15.6 77.7 %all-gather.5.cloned.1.call-done = bf16[128,4096]{1,0:T(8,128)(2,1)} async-done(((bf16[128,256]{1,0:T(8,128)(2,1)}), bf16[128,4096]{1,0:T(8,128)(2,1)}) %all-gather.5.cloned.1.call-update) | async-done | bytes 1048592 | tf_op jit(solution)/shard_map/all_gather | solution.py:20
  93.3 135.5 %all-gather.7.cloned.1.call-done = bf16[4096,3,256]{0,2,1:T(8,128)(2,1)} async-done(((bf16[512,3,256]{0,2,1:T(8,128)(2,1)}), bf16[4096,3,256]{0,2,1:T(8,128)(2,1)}) %all-gather.7.cloned.1.call-update) | async-done | bytes 6291472 | tf_op jit(solution)/shard_map/all_gather | solution.py:21
  228.8 5.3 %convolution_convert_fusion = bf16[128,768]{1,0:T(8,128)(2,1)S(1)} fusion(bf16[128,4096]{1,0:T(8,128)(2,1)} %all-gather.5.cloned.1.call-done, bf16[4096,768]{0,1:T(8,128)(2,1)} %bitcast.59), kind=kOutput, calls=%fused_computation.11 | convolution fusion | flops 805404672 | bytes 7536640 | tf_op jit(solution)/shard_map/dot_general | solution.py:23
  234.2 0.2 copy.81
  234.4 1.5 collective-permute-start
  235.9 0.7 copy.70
  236.6 9.2 %copy.65 = f32[64,64,256]{1,0,2:T(8,128)} copy(f32[64,64,256]{2,1,0:T(8,128)} %fusion.5) | data formatting | bytes 8388608 | tf_op jit(solution)/shard_map/tsk,kc->tsc/dot_general | solution.py:46
  245.8 0.2 copy.61
  246.0 0.2 maximum_convert_fusion
  246.1 1.5 fusion.21
  247.8 0.1 copy.64
  247.9 15.4 %fusion.32 = f32[256,2,64]{2,1,0:T(2,128)S(1)} fusion(f32[2,64,256]{1,0,2:T(2,128)S(1)} %copy.64, f32[64,64,256]{1,0,2:T(8,128)} %copy.65), kind=kOutput, calls=%fused_computation.61 | convolution fusion | flops 25165824 | bytes 4456448 | tf_op jit(solution)/shard_map/tsc,bsc->btc/dot_general | solution.py:47
  263.3 4.2 %multiply_reduce_fusion.1 = (f32[16,256]{0,1:T(8,128)}, f32[2,16,256]{1,0,2:T(2,128)S(1)}) fusion(f32[16,256]{0,1:T(8,128)S(1)} %copy.63, f32[2]{0:T(128)S(1)} %subtract_multiply_fusion, f32[2,64,256]{1,0,2:T(2,128)S(1)} %copy.64, f32[64]{0:T(128)S(1)} %broadcast_subtract_fusion), kind=kOutput, calls=%fused_computation.36 | convolution fusion | flops 6574080 | bytes 196872 | tf_op jit(solution)/shard_map/msc,bsc->bmc/dot_general | solution.py:49
  267.5 1.0 copy.68
  268.5 40.2 %all-gather = f32[128,256]{1,0:T(8,128)S(1)} all-gather(f32[16,256]{1,0:T(8,128)S(1)} %copy.68), channel_id=2, replica_groups=mesh['dp'=4,'seq'=8,'tensor'=16] {'seq'}, dimensions={0}, use_global_device_ids=true | all-gather | bytes 147456 | tf_op jit(solution)/shard_map/all_gather | solution.py:56
  309.0 0.1 copy.71
  309.2 3.7 fusion.12
  313.1 0.7 fusion.28
  313.9 82.1 %all-gather.9.cloned.1.call-done = bf16[128,4096]{0,1:T(8,128)(2,1)} async-done(((bf16[128,256]{0,1:T(8,128)(2,1)}), bf16[128,4096]{0,1:T(8,128)(2,1)}) %all-gather.9.cloned.1.call-update) | async-done | bytes 1048592 | tf_op jit(solution)/shard_map/all_gather | solution.py:75
  396.0 2.4 convolution_convert_fusion.1
  (43 shorter events, 1.1 us)
Async XLA Ops:
  6.5 389.5 %copy-start = (bf16[4096,256]{1,0:T(8,128)(2,1)S(1)}, bf16[4096,256]{1,0:T(8,128)(2,1)}, u32[]{:S(2)}) copy-start(bf16[4096,256]{1,0:T(8,128)(2,1)} %param.15) | copy-start | bytes 6291460
  6.5 3.2 copy-start.2
  6.5 3.2 copy-start.3
  6.5 5.1 %copy-start.1 = (f32[3,7,256]{2,1,0:T(8,128)S(1)}, f32[3,7,256]{2,1,0:T(8,128)}, u32[]{:S(2)}) copy-start(f32[3,7,256]{2,1,0:T(8,128)} %param.11) | copy-start | bytes 64516
  6.5 86.7 %all-gather.5.cloned.1.call-start = ((), (), s32[]{:S(2)}) async-start(), calls=%async_computation | async-start | bytes 1114112 | tf_op jit(solution)/shard_map/all_gather | solution.py:20
  7.3 221.6 %all-gather.7.cloned.1.call-start = ((), (), s32[]{:S(2)}) async-start(), calls=%async_computation.1 | async-start | bytes 7077888 | tf_op jit(solution)/shard_map/all_gather | solution.py:21
  9.7 386.4 %all-gather.9.cloned.1.call-start = ((), (), s32[]{:S(2)}) async-start(), calls=%async_computation.2 | async-start | bytes 1114112 | tf_op jit(solution)/shard_map/all_gather | solution.py:75
  234.4 11.6 %collective-permute-start = (bf16[6,3,256]{0,2,1:T(8,128)(2,1)S(1)}, bf16[6,3,256]{0,2,1:T(8,128)(2,1)S(1)}, u32[]{:S(2)}, u32[]{:S(2)}) collective-permute-start(bf16[6,3,256]{0,2,1:T(8,128)(2,1)S(1)} %bitcast.64), channel_id=1, source_target_pairs={{0,16},{16,32},{32,48},{48,64},{64,80},{80,96},{96,112},{1,17},{17... | collective-permute-start | bytes 27656 | tf_op jit(solution)/shard_map/ppermute | solution.py:13
  309.2 3.9 copy-start.4
Sparse Core Ops, SparseCore 0:
  10.5 82.7 all-gather.4
  95.4 133.4 all-gather.6
  314.0 81.9 all-gather.8
where the time goes:
time: 405 us
  waiting for transfers between devices  296 us (73%)
  blocking collectives  40.2 us (10%)
  matrix products  34.9 us (9%)
  local copies, waits for them, and re-layouts  14.5 us (4%)
  between operations  13.4 us (3%)
  other arithmetic  4.23 us (1%)
    all_gather x1, waiting for transfers between devices, body(): piece = lax.all_gather(in_weight, 'seq', axis=0, tiled=True)  136 us
    all_gather x1, waiting for transfers between devices, body(): lax.all_gather(gated, 'tensor', axis=1, tiled=True)  82.1 us
    all_gather x1, waiting for transfers between devices, body(): whole_feats = lax.all_gather(features, 'tensor', axis=1, tiled=True)  77.7 us
    all_gather x1, blocking collectives, body(): gathered_sums = lax.all_gather(device_sum, 'seq')  40.2 us
    dot_general x1, matrix products, body(): inner = jnp.einsum('tsc,bsc->btc', toeplitz, pieces, precision=precise)  15.4 us
    dot_general x1, local copies, waits for them, and re-layouts, body(): toeplitz = jnp.einsum('tsk,kc->tsc', select, kernel, precision=precise)  9.15 us
  transfers between devices with their start and end apart: 4, of which 3 were waited for; matrix products, arithmetic and copies ran while one was open for 4% of the time, Pallas kernels for 0%

commit v1 on v0

--- a/solution.py
+++ b/solution.py
@@ -72,7 +72,9 @@
     conv = (inner + outer).reshape(tok_rows, channels)
     gated = (short[:, 0, :] * (conv + skip_gain[None, :] * product)).astype(jnp.bfloat16)
     mixed = jnp.dot(
-        lax.all_gather(gated, "tensor", axis=1, tiled=True),
+        jnp.concatenate(
+            lax.all_to_all(jnp.stack([gated] * lax.axis_size("tensor")), "tensor", 0, 0), axis=1
+        ),
         out_weight,
         preferred_element_type=jnp.float32,
     )

time: 405 us -> 386 us (0.953)
  waiting for transfers between devices: 296 us -> 214 us
  blocking collectives: 40.2 us -> 104 us
    all_gather x1 -> x0, waiting for transfers between devices: 82.1 us -> none  [body(): lax.all_gather(gated, 'tensor', axis=1, tiled=True)]
    all_to_all x0 -> x1, blocking collectives: none -> 63.8 us  [body(): lax.all_to_all(jnp.stack([gated] * lax.axis_size('tensor')), 'tensor', 0, 0)]
  transfers between devices with their start and end apart: 4 -> 3, of which waited for: 3 -> 2; matrix products, arithmetic and copies ran while one was open for 4% -> 5% of each run, Pallas kernels for 0% -> 0%
where the time goes in v1:
time: 386 us; the launch traced here: 385 us
  waiting for transfers between devices  214 us (55%)
  blocking collectives  104 us (27%)
  matrix products  33.7 us (9%)
  local copies, waits for them, and re-layouts  14.7 us (4%)
  between operations  13.7 us (4%)
    all_gather x1, waiting for transfers between devices, body(): piece = lax.all_gather(in_weight, 'seq', axis=0, tiled=True)  136 us
    all_gather x1, waiting for transfers between devices, body(): whole_feats = lax.all_gather(features, 'tensor', axis=1, tiled=True)  77.8 us
    all_to_all x1, blocking collectives, body(): lax.all_to_all(jnp.stack([gated] * lax.axis_size('tensor')), 'tensor', 0, 0)  63.8 us
    all_gather x1, blocking collectives, body(): gathered_sums = lax.all_gather(device_sum, 'seq')  40.2 us
    dot_general x1, matrix products, body(): inner = jnp.einsum('tsc,bsc->btc', toeplitz, pieces, precision=precise)  15.4 us
    dot_general x1, local copies, waits for them, and re-layouts, body(): toeplitz = jnp.einsum('tsk,kc->tsc', select, kernel, precision=precise)  9.13 us
  transfers between devices with their start and end apart: 3, of which 2 were waited for; matrix products, arithmetic and copies ran while one was open for 5% of the time, Pallas kernels for 0%

profile of v1, /device:TPU:1, one launch (start us, length us, event | category | flops | bytes accessed | tf_op | source)
XLA Modules:
  0.0 385.3 jit_solution(14007306058301052159)
XLA Ops:
  6.6 0.7 all-gather.4.cloned.1.call-update
  7.3 2.3 copy.59
  10.0 1.6 multiply_reduce_fusion
  11.7 3.9 %fusion.5 = f32[64,64,256]{2,1,0:T(8,128)} fusion(s32[64,64]{1,0:T(8,128)S(1)} %iota_subtract_fusion, f32[256,64]{1,0:T(8,128)S(1)} %multiply_reduce_fusion), kind=kOutput, calls=%fused_computation.10 | convolution fusion | flops 805568512 | bytes 4276224 | tf_op jit(solution)/shard_map/tsk,kc->tsc/dot_general | solution.py:46
  15.5 77.8 %all-gather.4.cloned.1.call-done = bf16[128,4096]{1,0:T(8,128)(2,1)} async-done(((bf16[128,256]{1,0:T(8,128)(2,1)}), bf16[128,4096]{1,0:T(8,128)(2,1)}) %all-gather.4.cloned.1.call-update) | async-done | bytes 1048592 | tf_op jit(solution)/shard_map/all_gather | solution.py:20
  93.3 135.5 %all-gather.6.cloned.1.call-done = bf16[4096,3,256]{0,2,1:T(8,128)(2,1)} async-done(((bf16[512,3,256]{0,2,1:T(8,128)(2,1)}), bf16[4096,3,256]{0,2,1:T(8,128)(2,1)}) %all-gather.6.cloned.1.call-update) | async-done | bytes 6291472 | tf_op jit(solution)/shard_map/all_gather | solution.py:21
  228.8 5.3 %convolution_convert_fusion = bf16[128,768]{1,0:T(8,128)(2,1)S(1)} fusion(bf16[128,4096]{1,0:T(8,128)(2,1)} %all-gather.4.cloned.1.call-done, bf16[4096,768]{0,1:T(8,128)(2,1)} %bitcast.62), kind=kOutput, calls=%fused_computation.11 | convolution fusion | flops 805404672 | bytes 7536640 | tf_op jit(solution)/shard_map/dot_general | solution.py:23
  234.2 0.2 copy.81
  234.4 1.5 collective-permute-start
  235.9 0.8 copy.70
  236.6 9.1 %copy.65 = f32[64,64,256]{1,0,2:T(8,128)} copy(f32[64,64,256]{2,1,0:T(8,128)} %fusion.5) | data formatting | bytes 8388608 | tf_op jit(solution)/shard_map/tsk,kc->tsc/dot_general | solution.py:46
  245.8 0.2 copy.61
  245.9 0.2 maximum_convert_fusion
  246.1 1.5 fusion.21
  247.7 0.1 copy.64
  247.9 15.4 %fusion.32 = f32[256,2,64]{2,1,0:T(2,128)S(1)} fusion(f32[2,64,256]{1,0,2:T(2,128)S(1)} %copy.64, f32[64,64,256]{1,0,2:T(8,128)} %copy.65), kind=kOutput, calls=%fused_computation.61 | convolution fusion | flops 25165824 | bytes 4456448 | tf_op jit(solution)/shard_map/tsc,bsc->btc/dot_general | solution.py:47
  263.3 4.2 %multiply_reduce_fusion.1 = (f32[16,256]{0,1:T(8,128)}, f32[2,16,256]{1,0,2:T(2,128)S(1)}) fusion(f32[16,256]{0,1:T(8,128)S(1)} %copy.63, f32[2]{0:T(128)S(1)} %subtract_multiply_fusion, f32[2,64,256]{1,0,2:T(2,128)S(1)} %copy.64, f32[64]{0:T(128)S(1)} %broadcast_subtract_fusion), kind=kOutput, calls=%fused_computation.36 | convolution fusion | flops 6574080 | bytes 196872 | tf_op jit(solution)/shard_map/msc,bsc->bmc/dot_general | solution.py:49
  267.5 1.0 copy.68
  268.5 40.2 %all-gather = f32[128,256]{1,0:T(8,128)S(1)} all-gather(f32[16,256]{1,0:T(8,128)S(1)} %copy.68), channel_id=2, replica_groups=mesh['dp'=4,'seq'=8,'tensor'=16] {'seq'}, dimensions={0}, use_global_device_ids=true | all-gather | bytes 147456 | tf_op jit(solution)/shard_map/all_gather | solution.py:56
  309.0 0.1 copy.71
  309.1 3.7 fusion.12
  313.2 0.2 stack.2
  313.4 63.8 %all_to_all.5 = bf16[16,128,256]{1,2,0:T(8,128)(2,1)S(1)} all-to-all(bf16[16,128,256]{1,2,0:T(8,128)(2,1)S(1)} %stack.2), channel_id=1, replica_groups=mesh['dp'=4,'seq'=8,'tensor'=16] {'tensor'}, dimensions={0} | all-to-all | bytes 2097152 | tf_op jit(solution)/shard_map/all_to_all | solution.py:76
  377.2 1.2 convolution_convert_fusion.1
  (42 shorter events, 1.2 us)
Async XLA Ops:
  6.5 370.7 %copy-start = (bf16[4096,256]{1,0:T(8,128)(2,1)S(1)}, bf16[4096,256]{1,0:T(8,128)(2,1)}, u32[]{:S(2)}) copy-start(bf16[4096,256]{1,0:T(8,128)(2,1)} %param.15) | copy-start | bytes 6291460
  6.5 3.1 copy-start.2
  6.5 3.1 copy-start.3
  6.5 5.0 %copy-start.1 = (f32[3,7,256]{2,1,0:T(8,128)S(1)}, f32[3,7,256]{2,1,0:T(8,128)}, u32[]{:S(2)}) copy-start(f32[3,7,256]{2,1,0:T(8,128)} %param.11) | copy-start | bytes 64516
  6.5 86.7 %all-gather.4.cloned.1.call-start = ((), (), s32[]{:S(2)}) async-start(), calls=%async_computation.1 | async-start | bytes 1114112 | tf_op jit(solution)/shard_map/all_gather | solution.py:20
  7.3 221.5 %all-gather.6.cloned.1.call-start = ((), (), s32[]{:S(2)}) async-start(), calls=%async_computation.2 | async-start | bytes 7077888 | tf_op jit(solution)/shard_map/all_gather | solution.py:21
  234.4 11.6 %collective-permute-start = (bf16[6,3,256]{0,2,1:T(8,128)(2,1)S(1)}, bf16[6,3,256]{0,2,1:T(8,128)(2,1)S(1)}, u32[]{:S(2)}, u32[]{:S(2)}) collective-permute-start(bf16[6,3,256]{0,2,1:T(8,128)(2,1)S(1)} %bitcast.68), channel_id=1, source_target_pairs={{0,16},{16,32},{32,48},{48,64},{64,80},{80,96},{96,112},{1,17},{17... | collective-permute-start | bytes 27656 | tf_op jit(solution)/shard_map/ppermute | solution.py:13
  309.1 3.9 %copy-start.4 = (f32[256]{0:T(256)S(1)}, f32[256]{0:T(256)}, u32[]{:S(2)}) copy-start(f32[256]{0:T(256)} %param.14) | copy-start | bytes 3076
Sparse Core Ops, SparseCore 0:
  10.5 82.7 all-gather.3
  95.4 133.4 all-gather.5
